TPU v7x, 256 devices: a whole 4x4x8 slice. The times are simulated.
256 devices in a mesh: dp: 4 (over z_lo, core), cp: 16 (over y, z_hi), tp: 4 (over x).
Axes of the slice: x: 4, y: 4, z: 8 (z_hi: 4, z_lo: 2; z = z_hi * 2 + z_lo), core: 2. Of those that a mesh axis runs over, the one named last changes fastest.
Arguments:
- hidden: bfloat16 [4, 2048, 8192], P('dp', 'cp'), may hold values from -6 to 6
- query: bfloat16 [4, 2048, 8192], P('dp', 'cp', 'tp'), may hold values from -360 to 360
- grad_out: bfloat16 [4, 2048, 8192], P('dp', 'cp', 'tp'), may hold values from -6 to 6
- k_weight: bfloat16 [8192, 1024], P('dp', 'tp'), may hold values from -0.0625 to 0.0625
- v_weight: bfloat16 [8192, 1024], P('dp', 'tp'), may hold values from -0.0625 to 0.0625
- doc_starts: int32 [4, 4], P('dp'), may hold values from 0 to 2047, as said below
Outputs:
- attn_out: bfloat16 [4, 2048, 8192], P('dp', 'cp', 'tp')
- query_grad: bfloat16 [4, 2048, 8192], P('dp', 'cp', 'tp')
- k_weight_grad: float32 [8192, 1024], P(('dp', 'cp'), 'tp')
- v_weight_grad: float32 [8192, 1024], P(('dp', 'cp'), 'tp')
Inputs may be any that keep to these rules, and one draw needn't show every extreme that they name: `doc_starts`: in each sequence the starts strictly increase and the first is 0.
All inputs are finite; a program needn't handle non-finite values.
Results may differ from a plain program's by a relative error of at most 0.04.
The roundings to bfloat16 on the way count: a program that leaves them out, or rounds other values in their place, can miss the bound.
Values may be sent and summed in bfloat16 or wider, within the bound.
No kernel may reach another device: no remote copies, remote signals or barrier semaphores. Data moves between devices by JAX's collectives and lax.ppermute only.
A program may use at most 128 MiB of HBM per device.

v0:
```python
import jax
import jax.numpy as jnp
from jax import lax
from jax.sharding import PartitionSpec as P

DH = 128
NEG_BIG = -1e30


def place(rows, tok_rows, seq_rows):
    stretch = rows // tok_rows
    within = rows % tok_rows
    half_rows = tok_rows // 2
    return jnp.where(
        within < half_rows,
        stretch * half_rows + within,
        seq_rows - (stretch + 1) * half_rows + within - half_rows,
    )


def doc_index(positions, starts):
    return jnp.sum((starts[None, :] <= positions[:, None]).astype(jnp.int32), axis=1) - 1


def on_device(hidden, query, grad_out, k_weight, v_weight, doc_starts):
    inputs = hidden[0]
    tok_rows, width = inputs.shape
    cp_count = lax.axis_size("cp")
    dp_count = lax.axis_size("dp")
    seq_rows = tok_rows * cp_count
    score_scale = DH ** (-0.5)
    kv_width = k_weight.shape[1]
    kv_heads = kv_width // DH
    per_group = query.shape[2] // DH // kv_heads
    starts = doc_starts[0]
    blk = width // (dp_count * cp_count)
    cols = inputs.reshape(tok_rows, dp_count, cp_count, blk).transpose(2, 0, 1, 3)
    cols = lax.all_to_all(cols, "cp", 0, 0, tiled=True)
    both_w = jnp.concatenate([k_weight, v_weight], axis=1)
    both_w = lax.all_gather(both_w, "dp", axis=0, tiled=True)
    kv = jnp.dot(inputs, both_w, preferred_element_type=jnp.float32).astype(jnp.bfloat16)
    kv_all = lax.all_gather(kv, "cp", axis=0, tiled=True)
    key_heads = kv_all[:, :kv_width].reshape(seq_rows, kv_heads, DH)
    value_heads = kv_all[:, kv_width:].reshape(seq_rows, kv_heads, DH)
    own_rows = lax.axis_index("cp") * tok_rows + jnp.arange(tok_rows, dtype=jnp.int32)
    own_place = place(own_rows, tok_rows, seq_rows)
    own_doc = doc_index(own_place, starts)
    key_place = place(jnp.arange(seq_rows, dtype=jnp.int32), tok_rows, seq_rows)
    key_doc = doc_index(key_place, starts)
    allowed = (key_place[None, :] <= own_place[:, None]) & (key_doc[None, :] == own_doc[:, None])
    queries = query[0].reshape(tok_rows, kv_heads, per_group, DH)
    upstream = grad_out[0].reshape(tok_rows, kv_heads, per_group, DH)
    scores = (
        jnp.einsum("qgid,kgd->giqk", queries, key_heads, preferred_element_type=jnp.float32)
        * score_scale
    )
    scores = jnp.where(allowed, scores, NEG_BIG)
    top_score = jnp.max(scores, axis=-1)
    expos = jnp.where(allowed, jnp.exp(scores - top_score[..., None]), 0.0)
    log_total = top_score + jnp.log(jnp.sum(expos, axis=-1))
    weights = jnp.where(allowed, jnp.exp(scores - log_total[..., None]), 0.0)
    weights_bf = weights.astype(jnp.bfloat16)
    out_rows = jnp.einsum(
        "giqk,kgd->qgid", weights_bf, value_heads, preferred_element_type=jnp.float32
    ).astype(jnp.bfloat16)
    delta = jnp.transpose(
        jnp.sum(upstream.astype(jnp.float32) * out_rows.astype(jnp.float32), axis=-1), (1, 2, 0)
    )
    prob_grads = jnp.einsum(
        "qgid,kgd->giqk", upstream, value_heads, preferred_element_type=jnp.float32
    )
    score_grads = (weights * (prob_grads - delta[..., None])).astype(jnp.bfloat16)
    query_acc = (
        jnp.einsum("giqk,kgd->qgid", score_grads, key_heads, preferred_element_type=jnp.float32)
        * score_scale
    )
    key_term = (
        jnp.einsum("giqk,qgid->kgd", score_grads, queries, preferred_element_type=jnp.float32)
        * score_scale
    )
    value_term = jnp.einsum(
        "giqk,qgid->kgd", weights_bf, upstream, preferred_element_type=jnp.float32
    )
    both_terms = jnp.concatenate(
        [key_term.reshape(seq_rows, kv_width), value_term.reshape(seq_rows, kv_width)], axis=1
    ).astype(jnp.bfloat16)
    both_grads = lax.psum(both_terms, "cp")
    grads = both_grads.reshape(cp_count, tok_rows, 2 * kv_width)
    partial = jnp.einsum("ctjb,ctn->jbn", cols, grads, preferred_element_type=jnp.float32)
    result = lax.psum_scatter(partial, "dp", scatter_dimension=0, tiled=True)[0]
    attn_rows = out_rows.reshape(1, tok_rows, kv_heads * per_group * DH)
    query_rows = query_acc.astype(jnp.bfloat16).reshape(1, tok_rows, kv_heads * per_group * DH)
    return (attn_rows, query_rows, result[:, :kv_width], result[:, kv_width:])


def solution(mesh):
    placed = (
        P("dp", "cp", None),
        P("dp", "cp", "tp"),
        P("dp", "cp", "tp"),
        P("dp", "tp"),
        P("dp", "tp"),
        P("dp", None),
    )
    return jax.shard_map(
        on_device,
        mesh=mesh,
        in_specs=placed,
        out_specs=(
            P("dp", "cp", "tp"),
            P("dp", "cp", "tp"),
            P(("dp", "cp"), "tp"),
            P(("dp", "cp"), "tp"),
        ),
        check_vma=False,
    )
```

profile of v0, /device:TPU:1, one launch (start us, length us, event | category | flops | bytes accessed | tf_op | source)
XLA Modules:
  0.0 460.0 jit_solution(11077758612200397458)
XLA Ops:
  7.2 3.1 pad_maximum_fusion
  10.3 88.3 %all-gather.3.cloned.1.call-done = bf16[8192,512]{1,0:T(8,128)(2,1)} async-done(((bf16[2048,512]{1,0:T(8,128)(2,1)}), bf16[8192,512]{1,0:T(8,128)(2,1)}) %all-gather.3.cloned.1.call-update) | async-done | bytes 8388624 | tf_op jit(solution)/shard_map/all_gather | solution.py:40
  98.7 7.0 %fusion.18 = bf16[128,512]{0,1:T(8,128)(2,1)} fusion(bf16[8192,512]{1,0:T(8,128)(2,1)} %all-gather.3.cloned.1.call-done, bf16[1,128,8192]{2,1,0:T(8,128)(2,1)} %param.6), kind=kOutput, calls=%fused_computation.24 | convolution fusion | flops 1073807360 | bytes 10616832 | tf_op jit(solution)/shard_map/dot_general | solution.py:41
  105.7 3.3 copy.76
  109.0 2.6 copy.77
  111.6 8.4 %all-to-all-start = ((bf16[16,128,4,128]{3,1,2,0:T(8,128)(2,1)}), bf16[16,128,4,128]{3,1,2,0:T(8,128)(2,1)}, u32[]{:S(2)}, u32[]{:S(2)}) async-start(bf16[16,128,4,128]{3,1,2,0:T(8,128)(2,1)} %copy.77), calls=%async_computation | async-start | bytes 4194304 | tf_op jit(solution)/shard_map/all_to_all | solution.py:38
  120.3 0.3 copy.99
  120.6 1.0 copy.66
  121.9 1.3 compare_and_fusion
  123.2 66.3 %all-gather.5.cloned.1.call-done = bf16[2048,512]{0,1:T(8,128)(2,1)} async-done(((bf16[128,512]{0,1:T(8,128)(2,1)}), bf16[2048,512]{0,1:T(8,128)(2,1)}) %all-gather.5.cloned.1.call-update) | async-done | bytes 2097168 | tf_op jit(solution)/shard_map/all_gather | solution.py:42
  189.5 2.7 fusion.39
  192.2 2.6 fusion.3
  194.8 4.0 select_reduce_fusion
  198.8 1.7 copy-done
  200.6 8.2 %fusion.6 = bf16[2,2048,128]{1,2,0:T(8,128)(2,1)S(1)} fusion(bf16[128,2,8,128]{0,3,2,1:T(8,128)(2,1)S(1)} %bitcast.117, f32[2,2048,128,8]{2,1,3,0:T(8,128)} %copy-done, f32[2,8,128]{2,1,0:T(8,128)S(1)} %log_add_fusion, pred[128,2048]{0,1:T(8,128)(4,1)S(1)} %compare_and_fusion), kind=kOutput, calls=%fused_computation.12 | convolution fusion | flops 1095237632 | bytes 18620416 | tf_op jit(solution)/shard_map/giqk,qgid->kgd/dot_general | solution.py:81
  208.8 1.3 copy.74
  210.1 11.1 %multiply_reduce_fusion = (f32[128,2,8]{0,2,1:T(8,128)S(1)}, bf16[2,128,8,128]{3,1,2,0:T(8,128)(2,1)}) fusion(bf16[128,2,8,128]{0,3,2,1:T(8,128)(2,1)S(1)} %bitcast.118, bf16[2048,2,128,1]{0,2,3,1:T(8,128)(2,1)} %bitcast.114, f32[2,2048,128,8]{2,1,3,0:T(8,128)} %copy-done, f32[2,8,128]{2,1,0:T(8,128)S(1)} %log_add_fusion, ...), kind=kOutput, calls=%fused_computation.25 | convolution fusion | flops 1096022016 | bytes 19152896 | tf_op jit(solution)/shard_map/giqk,kgd->qgid/dot_general | solution.py:63
  221.3 9.3 %fusion.1 = bf16[2,8,128,2048]{2,3,1,0:T(8,128)(2,1)S(1)} fusion(f32[2,2048,128,8]{2,1,3,0:T(8,128)} %copy-done, f32[2,8,128]{2,1,0:T(8,128)S(1)} %bitcast.123, f32[2,8,128]{2,1,0:T(8,128)S(1)} %log_add_fusion, pred[128,2048]{0,1:T(8,128)(4,1)S(1)} %compare_and_fusion, bf16[2048,2,128,1]{0,2,3,1:T(8,128)(2,1)S(1)} %bitcast.115, ...), kind=kOutput, calls=%fused_computation.2 | convolution fusion | flops 1103101952 | bytes 27017216 | tf_op jit(solution)/shard_map/qgid,kgd->giqk/dot_general | solution.py:69
  230.5 3.2 copy-done.1
  233.7 2.8 fusion.5
  236.6 1.3 copy.73
  237.9 1.7 pad_maximum_fusion.1
  239.6 2.4 copy.75
  242.1 174.2 %all-reduce.2.cloned.1.call-done = bf16[16,128,512]{1,2,0:T(8,128)(2,1)} async-done(((bf16[16,128,512]{1,2,0:T(8,128)(2,1)}), bf16[16,128,512]{1,2,0:T(8,128)(2,1)}) %all-reduce.2.cloned.1.call-update) | async-done | bytes 2097168 | tf_op jit(solution)/shard_map/psum | solution.py:87
  416.3 4.4 fusion.11
  420.8 4.7 %fusion.14 = bf16[2,128,8,128]{3,1,2,0:T(8,128)(2,1)S(1)} fusion(bf16[2048,2,128,1]{0,2,3,1:T(8,128)(2,1)S(1)} %bitcast.106, bf16[2,8,128,2048]{2,3,1,0:T(8,128)(2,1)} %copy-done.1), kind=kOutput, calls=%fused_computation.21 | convolution fusion | flops 1074266112 | bytes 9961472 | tf_op jit(solution)/shard_map/giqk,kgd->qgid/dot_general | solution.py:74
  425.5 1.0 copy.80
  426.5 1.0 copy.79
  427.5 23.4 %reduce-scatter.2.cloned.1.call-done = f32[1,128,512]{1,2,0:T(8,128)} async-done(((f32[4,128,512]{1,2,0:T(8,128)}), f32[1,128,512]{1,2,0:T(8,128)}) %reduce-scatter.2.cloned.1.call-update) | async-done | bytes 262160 | tf_op jit(solution)/shard_map/reduce_scatter | solution.py:90
  451.0 1.0 fusion.40
  452.0 0.8 copy.81
  452.7 0.8 copy.82
  (30 shorter events, 0.7 us)
Async XLA Ops:
  7.2 91.5 %all-gather.3.cloned.1.call-start = ((), (), s32[]{:S(2)}) async-start(), calls=%async_computation.2 | async-start | bytes 10485760 | tf_op jit(solution)/shard_map/all_gather | solution.py:40
  10.3 179.2 %all-gather.5.cloned.1.call-start = ((), (), s32[]{:S(2)}) async-start(), calls=%async_computation.3 | async-start | bytes 2228224 | tf_op jit(solution)/shard_map/all_gather | solution.py:42
  105.7 14.6 %copy-start.3 = (bf16[1,128,2048]{2,1,0:T(8,128)(2,1)S(1)}, bf16[1,128,2048]{2,1,0:T(8,128)(2,1)}, u32[]{:S(2)}) copy-start(bf16[1,128,2048]{2,1,0:T(8,128)(2,1)} %param.7) | copy-start | bytes 1572868
  105.7 14.9 %copy-start.4 = (bf16[1,128,2048]{2,1,0:T(8,128)(2,1)S(1)}, bf16[1,128,2048]{2,1,0:T(8,128)(2,1)}, u32[]{:S(2)}) copy-start(bf16[1,128,2048]{2,1,0:T(8,128)(2,1)} %param.8) | copy-start | bytes 1572868
  105.7 16.0 %copy-start.7 = (s32[1,4]{1,0:T(1,128)S(1)}, s32[1,4]{1,0:T(1,128)}, u32[]{:S(2)}) copy-start(s32[1,4]{1,0:T(1,128)} %param.11) | copy-start | bytes 52
  111.6 130.4 %all-to-all-start = ((bf16[16,128,4,128]{3,1,2,0:T(8,128)(2,1)}), bf16[16,128,4,128]{3,1,2,0:T(8,128)(2,1)}, u32[]{:S(2)}, u32[]{:S(2)}) async-start(bf16[16,128,4,128]{3,1,2,0:T(8,128)(2,1)} %copy.77), calls=%async_computation | async-start | bytes 4194304 | tf_op jit(solution)/shard_map/all_to_all | solution.py:38
  120.1 296.2 %all-reduce.2.cloned.1.call-start = ((), (), s32[]{:S(2)}) async-start(), calls=%async_computation.4 | async-start | bytes 4194304 | tf_op jit(solution)/shard_map/psum | solution.py:87
  194.8 5.7 %copy-start = (f32[2,2048,128,8]{2,1,3,0:T(8,128)}, f32[2,2048,128,8]{2,1,3,0:T(8,128)S(1)}, u32[]{:S(2)}) copy-start(f32[2,2048,128,8]{2,1,3,0:T(8,128)S(1)} %get-tuple-element.25) | copy-start | bytes 50331652
  194.8 5.7 %copy-start.6 = (bf16[1,128,2048]{1,2,0:T(8,128)(2,1)S(1)}, bf16[1,128,2048]{1,2,0:T(8,128)(2,1)}, u32[]{:S(2)}) copy-start(bf16[1,128,2048]{1,2,0:T(8,128)(2,1)} %copy.66) | copy-start | bytes 1572868
  210.1 11.1 %copy-start.2 = (bf16[2048,256]{0,1:T(8,128)(2,1)S(1)}, bf16[2048,256]{0,1:T(8,128)(2,1)}, u32[]{:S(2)}) copy-start(bf16[2048,256]{0,1:T(8,128)(2,1)} %get-tuple-element.21) | copy-start | bytes 3145732
  230.5 3.2 copy-start.1
  242.0 208.9 %reduce-scatter.2.cloned.1.call-start = ((), (), s32[]{:S(2)}) async-start(), calls=%async_computation.5 | async-start | bytes 1310720 | tf_op jit(solution)/shard_map/reduce_scatter | solution.py:90
  420.8 5.7 %copy-start.5 = (bf16[2,128,8,128]{3,1,2,0:T(8,128)(2,1)S(1)}, bf16[2,128,8,128]{3,1,2,0:T(8,128)(2,1)}, u32[]{:S(2)}) copy-start(bf16[2,128,8,128]{3,1,2,0:T(8,128)(2,1)} %get-tuple-element.27) | copy-start | bytes 1572868
Sparse Core Ops, SparseCore 0:
  10.4 88.2 all-gather.2
  105.8 83.6 all-gather.4
  242.2 174.1 all-reduce.1
  420.9 30.0 reduce-scatter.1
where the time goes:
time: 460 us
  waiting for transfers between devices  352 us (77%)
  matrix products  50.2 us (11%)
  local copies, waits for them, and re-layouts  24.5 us (5%)
  between operations  14 us (3%)
  other arithmetic  10.3 us (2%)
  starting transfers between devices  8.78 us (2%)
    psum x1, waiting for transfers between devices, on_device(): both_grads = lax.psum(both_terms, 'cp')  174 us
    all_gather x1, waiting for transfers between devices, on_device(): both_w = lax.all_gather(both_w, 'dp', axis=0, tiled=True)  88.3 us
    all_gather x1, waiting for transfers between devices, on_device(): kv_all = lax.all_gather(kv, 'cp', axis=0, tiled=True)  66.3 us
    reduce_scatter x1, waiting for transfers between devices, on_device(): result = lax.psum_scatter(partial, 'dp', scatter_dimension=0, tiled=True)[0]  23.4 us
    unnamed x22, local copies, waits for them, and re-layouts  12.8 us
    dot_general x1, matrix products, on_device(): jnp.einsum('giqk,kgd->qgid', weights_bf, value_heads, preferred_element_t...  11.1 us
    dot_general x1, matrix products, on_device(): jnp.einsum('qgid,kgd->giqk', upstream, value_heads, preferred_element_typ...  9.25 us
  transfers between devices with their start and end apart: 5, of which 4 were waited for; matrix products, arithmetic and copies ran while one was open for 14% of the time, Pallas kernels for 0%

commit v1 on v0

--- a/solution.py
+++ b/solution.py
@@ -1,3 +1,4 @@
+import functools
 import jax
 import jax.numpy as jnp
 from jax import lax
@@ -5,6 +6,15 @@
 
 DH = 128
 NEG_BIG = -1e30
+
+
+def see_the_flows(patch, link_axis):
+    return jnp.concatenate(
+        lax.all_to_all(jnp.stack([patch] * lax.axis_size(link_axis)), link_axis, 0, 0), axis=0
+    )
+
+
+play_circles = functools.partial(see_the_flows, link_axis="cp")
 
 
 def place(rows, tok_rows, seq_rows):
@@ -39,7 +49,7 @@
     both_w = jnp.concatenate([k_weight, v_weight], axis=1)
     both_w = lax.all_gather(both_w, "dp", axis=0, tiled=True)
     kv = jnp.dot(inputs, both_w, preferred_element_type=jnp.float32).astype(jnp.bfloat16)
-    kv_all = lax.all_gather(kv, "cp", axis=0, tiled=True)
+    kv_all = play_circles(kv)
     key_heads = kv_all[:, :kv_width].reshape(seq_rows, kv_heads, DH)
     value_heads = kv_all[:, kv_width:].reshape(seq_rows, kv_heads, DH)
     own_rows = lax.axis_index("cp") * tok_rows + jnp.arange(tok_rows, dtype=jnp.int32)

time: 460 us -> 441 us (0.959)
  waiting for transfers between devices: 352 us -> 324 us
  starting transfers between devices: 8.78 us -> 13.4 us
    all_gather x1 -> x0, waiting for transfers between devices: 66.3 us -> none  [on_device(): kv_all = lax.all_gather(kv, 'cp', axis=0, tiled=True)]
    all_to_all x0 -> x1, waiting for transfers between devices: none -> 38.9 us  [see_the_flows(): lax.all_to_all(jnp.stack([patch] * lax.axis_size(link_axis)), link_axis,...]
    all_to_all x0 -> x1, starting transfers between devices: none -> 8.39 us  [see_the_flows(): lax.all_to_all(jnp.stack([patch] * lax.axis_size(link_axis)), link_axis,...]
  transfers between devices with their start and end apart: 5 -> 5, of which waited for: 4 -> 4; matrix products, arithmetic and copies ran while one was open for 14% -> 15% of each run, Pallas kernels for 0% -> 0%
where the time goes in v1:
time: 441 us; the launch traced here: 440 us
  waiting for transfers between devices  324 us (73%)
  matrix products  52.1 us (12%)
  local copies, waits for them, and re-layouts  26.7 us (6%)
  between operations  14 us (3%)
  starting transfers between devices  13.4 us (3%)
  other arithmetic  10.4 us (2%)
    psum x1, waiting for transfers between devices, on_device(): both_grads = lax.psum(both_terms, 'cp')  173 us
    all_gather x1, waiting for transfers between devices, on_device(): both_w = lax.all_gather(both_w, 'dp', axis=0, tiled=True)  88.4 us
    all_to_all x1, waiting for transfers between devices, see_the_flows(): lax.all_to_all(jnp.stack([patch] * lax.axis_size(link_axis)), link_axis,...  38.9 us
    reduce_scatter x1, waiting for transfers between devices, on_device(): result = lax.psum_scatter(partial, 'dp', scatter_dimension=0, tiled=True)[0]  23.4 us
    unnamed x22, local copies, waits for them, and re-layouts  13.4 us
    dot_general x1, matrix products, on_device(): jnp.einsum('giqk,kgd->qgid', weights_bf, value_heads, preferred_element_t...  10.8 us
    dot_general x1, matrix products, on_device(): jnp.einsum('giqk,qgid->kgd', weights_bf, upstream, preferred_element_type...  10.1 us
    dot_general x1, matrix products, on_device(): jnp.einsum('qgid,kgd->giqk', upstream, value_heads, preferred_element_typ...  9.28 us
  transfers between devices with their start and end apart: 5, of which 4 were waited for; matrix products, arithmetic and copies ran while one was open for 15% of the time, Pallas kernels for 0%

profile of v1, /device:TPU:1, one launch (start us, length us, event | category | flops | bytes accessed | tf_op | source)
XLA Modules:
  0.0 440.4 jit_solution(13827910349693783425)
XLA Ops:
  7.2 3.0 pad_maximum_fusion
  10.3 88.4 %all-gather.2.cloned.1.call-done = bf16[8192,512]{1,0:T(8,128)(2,1)} async-done(((bf16[2048,512]{1,0:T(8,128)(2,1)}), bf16[8192,512]{1,0:T(8,128)(2,1)}) %all-gather.2.cloned.1.call-update) | async-done | bytes 8388624 | tf_op jit(solution)/shard_map/all_gather | solution.py:50
  98.6 6.3 %fusion.18 = bf16[128,512]{0,1:T(8,128)(2,1)S(1)} fusion(bf16[8192,512]{1,0:T(8,128)(2,1)} %all-gather.2.cloned.1.call-done, bf16[1,128,8192]{2,1,0:T(8,128)(2,1)} %param.6), kind=kOutput, calls=%fused_computation.25 | convolution fusion | flops 1073807360 | bytes 10616832 | tf_op jit(solution)/shard_map/dot_general | solution.py:51
  105.0 1.7 stack.2
  106.8 8.4 %all-to-all-start = ((bf16[16,128,512]{1,2,0:T(8,128)(2,1)}), bf16[16,128,512]{1,2,0:T(8,128)(2,1)S(1)}, u32[]{:S(2)}, u32[]{:S(2)}) async-start(bf16[16,128,512]{1,2,0:T(8,128)(2,1)} %stack.2), calls=%async_computation | async-start | bytes 4194304 | tf_op jit(solution)/shard_map/all_to_all | solution.py:13
  115.2 4.1 copy.78
  119.2 1.0 copy.101
  120.2 1.0 copy.68
  121.2 3.9 copy.79
  125.4 1.3 compare_and_fusion
  126.8 38.9 %all-to-all-done = bf16[16,128,512]{1,2,0:T(8,128)(2,1)S(1)} async-done(((bf16[16,128,512]{1,2,0:T(8,128)(2,1)}), bf16[16,128,512]{1,2,0:T(8,128)(2,1)S(1)}, u32[]{:S(2)}, u32[]{:S(2)}) %all-to-all-start) | async-done | bytes 2097184 | tf_op jit(solution)/shard_map/all_to_all | solution.py:13
  165.6 4.9 %all-to-all-start.1 = ((bf16[16,128,4,128]{3,1,2,0:T(8,128)(2,1)}), bf16[16,128,4,128]{3,1,2,0:T(8,128)(2,1)}, u32[]{:S(2)}, u32[]{:S(2)}) async-start(bf16[16,128,4,128]{3,1,2,0:T(8,128)(2,1)} %copy.79), calls=%async_computation.1 | async-start | bytes 4194304 | tf_op jit(solution)/shard_map/all_to_all | solution.py:48
  171.0 3.6 fusion.3
  174.6 4.2 select_reduce_fusion
  178.8 1.5 copy-done
  180.4 10.1 %fusion.6 = bf16[2,2048,128]{1,2,0:T(8,128)(2,1)S(1)} fusion(bf16[128,2,8,128]{0,3,2,1:T(8,128)(2,1)} %bitcast.121, f32[2,2048,128,8]{2,1,3,0:T(8,128)} %copy-done, f32[2,8,128]{2,1,0:T(8,128)S(1)} %log_add_fusion, pred[128,2048]{0,1:T(8,128)(4,1)S(1)} %compare_and_fusion), kind=kOutput, calls=%fused_computation.12 | convolution fusion | flops 1095237632 | bytes 18620416 | tf_op jit(solution)/shard_map/giqk,qgid->kgd/dot_general | solution.py:91
  190.4 1.3 copy.76
  191.8 10.8 %multiply_reduce_fusion = (f32[128,2,8]{0,2,1:T(8,128)S(1)}, bf16[2,128,8,128]{3,1,2,0:T(8,128)(2,1)}) fusion(bf16[128,2,8,128]{0,3,2,1:T(8,128)(2,1)} %bitcast.122, bf16[2048,2,128,1]{0,2,3,1:T(8,128)(2,1)S(1)} %bitcast.119, f32[2,2048,128,8]{2,1,3,0:T(8,128)} %copy-done, f32[2,8,128]{2,1,0:T(8,128)S(1)} %log_add_fusion, ...), kind=kOutput, calls=%fused_computation.26 | convolution fusion | flops 1096022016 | bytes 19152896 | tf_op jit(solution)/shard_map/giqk,kgd->qgid/dot_general | solution.py:73
  202.6 9.3 %fusion.1 = bf16[2,8,128,2048]{2,3,1,0:T(8,128)(2,1)S(1)} fusion(f32[2,2048,128,8]{2,1,3,0:T(8,128)} %copy-done, f32[2,8,128]{2,1,0:T(8,128)S(1)} %bitcast.128, f32[2,8,128]{2,1,0:T(8,128)S(1)} %log_add_fusion, pred[128,2048]{0,1:T(8,128)(4,1)S(1)} %compare_and_fusion, bf16[2048,2,128,1]{0,2,3,1:T(8,128)(2,1)S(1)} %bitcast.120, ...), kind=kOutput, calls=%fused_computation.2 | convolution fusion | flops 1103101952 | bytes 27017216 | tf_op jit(solution)/shard_map/qgid,kgd->giqk/dot_general | solution.py:79
  211.9 3.2 copy-done.1
  215.1 2.8 fusion.5
  217.9 1.3 copy.75
  219.3 1.7 pad_maximum_fusion.1
  221.0 2.6 copy.77
  223.6 173.1 %all-reduce.2.cloned.1.call-done = bf16[16,128,512]{1,2,0:T(8,128)(2,1)} async-done(((bf16[16,128,512]{1,2,0:T(8,128)(2,1)}), bf16[16,128,512]{1,2,0:T(8,128)(2,1)}) %all-reduce.2.cloned.1.call-update) | async-done | bytes 2097168 | tf_op jit(solution)/shard_map/psum | solution.py:97
  396.7 4.4 %fusion.11 = f32[4,128,512]{1,2,0:T(8,128)} fusion(bf16[16,128,4,128]{3,1,2,0:T(8,128)(2,1)} %all-to-all-done.1, bf16[16,128,512]{1,2,0:T(8,128)(2,1)} %all-reduce.2.cloned.1.call-done), kind=kOutput, calls=%fused_computation.20 | convolution fusion | flops 1073741824 | bytes 5242880 | tf_op jit(solution)/shard_map/ctjb,ctn->jbn/dot_general | solution.py:99
  401.2 4.7 %fusion.14 = bf16[2,128,8,128]{3,1,2,0:T(8,128)(2,1)S(1)} fusion(bf16[2048,2,128,1]{0,2,3,1:T(8,128)(2,1)S(1)} %bitcast.111, bf16[2,8,128,2048]{2,3,1,0:T(8,128)(2,1)} %copy-done.1), kind=kOutput, calls=%fused_computation.22 | convolution fusion | flops 1074266112 | bytes 9961472 | tf_op jit(solution)/shard_map/giqk,kgd->qgid/dot_general | solution.py:84
  405.9 1.0 copy.82
  406.9 1.0 copy.81
  408.0 23.4 %reduce-scatter.2.cloned.1.call-done = f32[1,128,512]{1,2,0:T(8,128)} async-done(((f32[4,128,512]{1,2,0:T(8,128)}), f32[1,128,512]{1,2,0:T(8,128)}) %reduce-scatter.2.cloned.1.call-update) | async-done | bytes 262160 | tf_op jit(solution)/shard_map/reduce_scatter | solution.py:100
  431.4 1.0 fusion.40
  432.4 0.8 copy.83
  (31 shorter events, 1.6 us)
Async XLA Ops:
  7.2 91.5 %all-gather.2.cloned.1.call-start = ((), (), s32[]{:S(2)}) async-start(), calls=%async_computation.3 | async-start | bytes 10485760 | tf_op jit(solution)/shard_map/all_gather | solution.py:50
  105.0 14.2 %copy-start.3 = (bf16[1,128,2048]{2,1,0:T(8,128)(2,1)S(1)}, bf16[1,128,2048]{2,1,0:T(8,128)(2,1)}, u32[]{:S(2)}) copy-start(bf16[1,128,2048]{2,1,0:T(8,128)(2,1)} %param.7) | copy-start | bytes 1572868
  105.0 15.2 %copy-start.4 = (bf16[1,128,2048]{2,1,0:T(8,128)(2,1)S(1)}, bf16[1,128,2048]{2,1,0:T(8,128)(2,1)}, u32[]{:S(2)}) copy-start(bf16[1,128,2048]{2,1,0:T(8,128)(2,1)} %param.8) | copy-start | bytes 1572868
  105.0 20.2 %copy-start.7 = (s32[1,4]{1,0:T(1,128)S(1)}, s32[1,4]{1,0:T(1,128)}, u32[]{:S(2)}) copy-start(s32[1,4]{1,0:T(1,128)} %param.11) | copy-start | bytes 52
  106.8 58.8 %all-to-all-start = ((bf16[16,128,512]{1,2,0:T(8,128)(2,1)}), bf16[16,128,512]{1,2,0:T(8,128)(2,1)S(1)}, u32[]{:S(2)}, u32[]{:S(2)}) async-start(bf16[16,128,512]{1,2,0:T(8,128)(2,1)} %stack.2), calls=%async_computation | async-start | bytes 4194304 | tf_op jit(solution)/shard_map/all_to_all | solution.py:13
  165.6 58.0 %all-to-all-start.1 = ((bf16[16,128,4,128]{3,1,2,0:T(8,128)(2,1)}), bf16[16,128,4,128]{3,1,2,0:T(8,128)(2,1)}, u32[]{:S(2)}, u32[]{:S(2)}) async-start(bf16[16,128,4,128]{3,1,2,0:T(8,128)(2,1)} %copy.79), calls=%async_computation.1 | async-start | bytes 4194304 | tf_op jit(solution)/shard_map/all_to_all | solution.py:48
  170.5 226.3 %all-reduce.2.cloned.1.call-start = ((), (), s32[]{:S(2)}) async-start(), calls=%async_computation.4 | async-start | bytes 4194304 | tf_op jit(solution)/shard_map/psum | solution.py:97
  174.6 5.7 %copy-start = (f32[2,2048,128,8]{2,1,3,0:T(8,128)}, f32[2,2048,128,8]{2,1,3,0:T(8,128)S(1)}, u32[]{:S(2)}) copy-start(f32[2,2048,128,8]{2,1,3,0:T(8,128)S(1)} %get-tuple-element.25) | copy-start | bytes 50331652
  191.8 10.8 %copy-start.5 = (bf16[1,128,2048]{1,2,0:T(8,128)(2,1)S(1)}, bf16[1,128,2048]{1,2,0:T(8,128)(2,1)}, u32[]{:S(2)}) copy-start(bf16[1,128,2048]{1,2,0:T(8,128)(2,1)} %copy.68) | copy-start | bytes 1572868
  202.6 12.5 %copy-start.2 = (bf16[1,128,2048]{1,2,0:T(8,128)(2,1)S(1)}, bf16[1,128,2048]{1,2,0:T(8,128)(2,1)}, u32[]{:S(2)}) copy-start(bf16[1,128,2048]{1,2,0:T(8,128)(2,1)} %copy.101) | copy-start | bytes 1572868
  211.9 3.2 copy-start.1
  223.6 207.8 %reduce-scatter.2.cloned.1.call-start = ((), (), s32[]{:S(2)}) async-start(), calls=%async_computation.5 | async-start | bytes 1310720 | tf_op jit(solution)/shard_map/reduce_scatter | solution.py:100
  401.2 5.7 %copy-start.6 = (bf16[2,128,8,128]{3,1,2,0:T(8,128)(2,1)S(1)}, bf16[2,128,8,128]{3,1,2,0:T(8,128)(2,1)}, u32[]{:S(2)}) copy-start(bf16[2,128,8,128]{3,1,2,0:T(8,128)(2,1)} %get-tuple-element.27) | copy-start | bytes 1572868
Sparse Core Ops, SparseCore 0:
  10.4 88.2 all-gather.1
  223.7 172.9 all-reduce.1
  401.3 30.0 reduce-scatter.1
